TPU v7x, 512 devices: a whole 4x4x16 slice. The times are simulated.
512 devices in a mesh: sub: 128 (over y, z, core), case: 4 (over x).
Axes of the slice: x: 4, y: 4, z: 16, core: 2. Of those that a mesh axis runs over, the one named last changes fastest.
Arguments:
- load_interior: float32 [128, 128, 4096], P('sub', None, 'case'), may hold values from -6 to 6
- load_boundary: float32 [128, 128, 1024], P('sub', None, 'case'), may hold values from -6 to 6
- cond_blocks: float32 [128, 128, 4096], P('sub', 'case'), may hold values from -0.25 to 0.25
- block_rows: int32 [128, 128], P('sub', 'case'), may hold values from 0 to 15
- block_cols: int32 [128, 128], P('sub', 'case'), may hold values from 0 to 63, as said below
- interface_maps: int32 [128, 7, 2, 1024], P('sub'), may hold values from 0 to 1023, as said below
- merge_maps: float32 [128, 7, 1024, 512], P('sub', None, 'case'), as said below
Outputs:
- leaf_loads: float32 [128, 1024, 128], P('sub', 'case')
- node_loads: float32 [128, 1024, 128], P('sub', 'case')
Inputs may be any that keep to these rules, and one draw needn't show every extreme that they name: `block_cols`: entry k of a substructure's row lies in [(k // 32) * 16, (k // 32 + 1) * 16); blocks may repeat. `interface_maps`: each row of 1024 entries is a permutation; at level index l, slots that agree in all but their lowest l + 1 bits hold equal entries. `merge_maps`: at level index l, slots that agree in all but their lowest l + 1 bits hold equal entries.
All inputs are finite; a program needn't handle non-finite values.
Results may differ from a plain program's by a relative error of at most 0.0003.
Values sent between devices are 32-bit elements; how exact they have to be, the bound alone decides.
No kernel may reach another device: no remote copies, remote signals or barrier semaphores. Data moves between devices by JAX's collectives and lax.ppermute only.
A program may use at most 64 MiB of HBM per device.

v0:
```python
import jax
import jax.numpy as jnp
from jax import lax
from jax.sharding import PartitionSpec as P

BLK = 64


def from_partner(value, axis, distance):
    mask = 2**distance
    pairs = [(source, source ^ mask) for source in range(lax.axis_size(axis))]
    return lax.ppermute(value, axis, pairs)


def to_row_quarters(value):
    return lax.all_to_all(value, "case", split_axis=0, concat_axis=1, tiled=True)


def on_device(
    load_interior, load_boundary, cond_blocks, block_rows, block_cols, interface_maps, merge_maps
):
    groups = lax.axis_size("case")
    local_rows = load_interior.shape[2]
    quarter = load_boundary.shape[2]
    full_rows = quarter * groups
    interior_rows = local_rows * groups
    block_size = BLK
    blocks = lax.all_gather(cond_blocks[0], "case", axis=0, tiled=True)
    rows_of_blocks = lax.all_gather(block_rows[0], "case", axis=0, tiled=True)
    cols_of_blocks = lax.all_gather(block_cols[0], "case", axis=0, tiled=True)
    block_count = blocks.shape[0]
    blocks = blocks.reshape(block_count, block_size, block_size)
    joined = jnp.concatenate([load_interior, load_boundary], axis=2)
    joined = lax.all_to_all(joined, "sub", split_axis=1, concat_axis=0, tiled=True)[:, 0, :]
    joined = lax.all_to_all(joined, "case", split_axis=0, concat_axis=1, tiled=True)
    num_cases = joined.shape[0]
    parts = joined.reshape(num_cases, groups, local_rows + quarter)
    interior = jnp.transpose(parts[:, :, :local_rows].reshape(num_cases, interior_rows))
    boundary = jnp.transpose(parts[:, :, local_rows:].reshape(num_cases, full_rows))
    pieces = jnp.take(
        interior.reshape(interior_rows // block_size, block_size, num_cases), cols_of_blocks, axis=0
    )
    products = jnp.einsum("krc,kcn->krn", blocks, pieces, precision=lax.Precision.HIGH)
    row_blocks = full_rows // block_size
    onehot = (rows_of_blocks[None, :] == jnp.arange(row_blocks, dtype=jnp.int32)[:, None]).astype(
        jnp.float32
    )
    summed = jnp.dot(
        onehot, products.reshape(block_count, block_size * num_cases), precision=lax.Precision.HIGH
    )
    leaf = boundary - summed.reshape(full_rows, num_cases)
    leaf_share = to_row_quarters(leaf)
    slot = lax.axis_index("sub")
    levels = lax.axis_size("sub").bit_length() - 1
    current = leaf
    nodes = jnp.zeros_like(leaf)
    for level in range(1, levels + 1):
        half = 1 << level - 1
        maps = interface_maps[0, level - 1]
        matrix = lax.all_gather(merge_maps[0, level - 1], "case", axis=0, tiled=True)
        shared_rows = matrix.shape[1]
        upper = slot // half % 2 == 1
        other = from_partner(current, "sub", level - 1)
        stacked = jnp.concatenate([current, other], axis=0)

        def left_index(index):
            return jnp.where(upper, index + full_rows, index)

        def right_index(index):
            return jnp.where(upper, index, index + full_rows)

        shared = jnp.take(stacked, left_index(maps[0, :shared_rows]), axis=0) + jnp.take(
            stacked, right_index(maps[1, :shared_rows]), axis=0
        )
        kept_index = jnp.concatenate(
            [left_index(maps[0, shared_rows:]), right_index(maps[1, shared_rows:])]
        )
        parent = jnp.take(stacked, kept_index, axis=0) - jnp.dot(
            matrix, shared, precision=lax.Precision.HIGH
        )
        is_node = slot % (2 * half) == half
        if level == levels:
            is_node = jnp.logical_or(is_node, slot == 0)
        nodes = jnp.where(is_node, parent, nodes)
        current = parent
    return (leaf_share[None], to_row_quarters(nodes)[None])


def solution(mesh):
    placed = (
        P("sub", None, "case"),
        P("sub", None, "case"),
        P("sub", "case", None),
        P("sub", "case"),
        P("sub", "case"),
        P("sub", None, None, None),
        P("sub", None, "case", None),
    )
    return jax.shard_map(
        on_device,
        mesh=mesh,
        in_specs=placed,
        out_specs=(P("sub", "case", None), P("sub", "case", None)),
        check_vma=False,
    )
```

profile of v0, /device:TPU:8, one launch (start us, length us, event | category | flops | bytes accessed | tf_op | source)
XLA Modules:
  0.0 363.9 jit_solution(5309197116855584580)
XLA Ops:
  7.2 2.4 copy.236
  9.6 3.9 %fusion.110 = (f32[1,1,256,512]{3,2,1,0:T(8,128)}, f32[1,1,256,512]{3,2,1,0:T(8,128)}, f32[1,1,256,512]{3,2,1,0:T(8,128)}, f32[1,1,256,512]{3,2,1,0:T(8,128)}, f...) fusion(f32[1,7,256,512]{3,2,1,0:T(8,128)} %param.17), kind=kLoop, calls=%fused_computation.216 | loop fusion | bytes 7340032 | tf_op jit(solution)/shard_map/slice | solution.py:60
  16.9 1.5 copy.232
  18.4 19.6 %all-to-all-start = ((f32[1,128,1280]{2,0,1:T(1,128)}), f32[1,128,1280]{2,0,1:T(1,128)S(1)}, u32[]{:S(2)}, u32[]{:S(2)}) async-start(f32[1,128,1280]{2,0,1:T(1,128)} %copy.232), calls=%async_computation | async-start | bytes 1310720 | tf_op jit(solution)/shard_map/all_to_all | solution.py:34
  38.8 1.3 dynamic-slice
  40.9 9.0 %all-reduce.2 = (s32[128]{0:T(128)S(1)}, s32[128]{0:T(128)S(1)}) all-reduce(s32[128]{0:T(128)S(1)} %bitcast_dynamic-update-slice_fusion, s32[128]{0:T(128)S(1)} %bitcast_dynamic-update-slice_fusion.1), channel_id=3, replica_groups=mesh['sub'=128,'case'=4] {'case'}, use_global_device_ids=true, to_apply=%add.1 | all-reduce | flops 256 | bytes 2048 | tf_op jit(solution)/shard_map/all_gather | solution.py:30
  50.8 26.4 %all-to-all-done = f32[1,128,1280]{2,0,1:T(1,128)S(1)} async-done(((f32[1,128,1280]{2,0,1:T(1,128)}), f32[1,128,1280]{2,0,1:T(1,128)S(1)}, u32[]{:S(2)}, u32[]{:S(2)}) %all-to-all-start) | async-done | bytes 655392 | tf_op jit(solution)/shard_map/all_to_all | solution.py:34
  78.2 4.3 %all-to-all-start.1 = ((f32[4,32,1280]{2,1,0:T(8,128)}), f32[4,32,1280]{2,1,0:T(8,128)S(1)}, u32[]{:S(2)}, u32[]{:S(2)}) async-start(f32[4,32,1280]{2,1,0:T(8,128)} %bitcast.67), calls=%async_computation.1 | async-start | bytes 1310720 | tf_op jit(solution)/shard_map/all_to_all | solution.py:35
  82.5 18.3 %all-to-all-done.1 = f32[4,32,1280]{2,1,0:T(8,128)S(1)} async-done(((f32[4,32,1280]{2,1,0:T(8,128)}), f32[4,32,1280]{2,1,0:T(8,128)S(1)}, u32[]{:S(2)}, u32[]{:S(2)}) %all-to-all-start.1) | async-done | bytes 655392 | tf_op jit(solution)/shard_map/all_to_all | solution.py:35
  103.9 5.6 %copy.237 = f32[1,128,4096]{1,2,0:T(8,128)} copy(f32[1,128,4096]{2,0,1:T(1,128)} %all-gather.19.cloned.1.call-done) | data formatting | bytes 4194304 | tf_op jit(solution)/shard_map/all_gather | solution.py:28
  109.5 5.6 %copy.238 = f32[128,64,64]{2,1,0:T(8,128)} copy(f32[128,64,64]{0,2,1:T(8,128)} %bitcast.158) | data formatting | bytes 4194304 | tf_op jit(solution)/shard_map/reshape | solution.py:32
  115.1 7.0 %fusion.16 = f32[128,64,32]{1,2,0:T(8,128)} fusion(f32[128,64,64]{2,1,0:T(8,128)} %copy.238, f32[128,64,32]{1,2,0:T(8,128)S(1)} %gather_fusion, pred[128]{0:T(512)(128)(4,1)S(1)} %compare_and_fusion.21), kind=kOutput, calls=%fused_computation.38 | convolution fusion | flops 100925440 | bytes 4194432 | tf_op jit(solution)/shard_map/krc,kcn->krn/dot_general | solution.py:43
  122.1 3.1 copy.239
  125.8 1.9 collective-permute-start
  127.8 1.8 collective-permute-done
  129.7 2.8 gather_fusion.1
  134.8 2.9 select_subtract_fusion
  137.8 3.2 collective-permute-start.1
  141.0 4.2 %collective-permute-done.1 = f32[1024,32]{0,1:T(8,128)S(1)} collective-permute-done((f32[1024,32]{0,1:T(8,128)S(1)}, f32[1024,32]{0,1:T(8,128)S(1)}, u32[]{:S(2)}, u32[]{:S(2)}) %collective-permute-start.1) | collective-permute-done | bytes 131104 | tf_op jit(solution)/shard_map/ppermute | solution.py:12
  145.5 2.8 gather_fusion.4
  150.6 2.9 fusion.25
  153.5 2.2 collective-permute-start.2
  155.8 8.0 %collective-permute-done.2 = f32[1024,32]{0,1:T(8,128)S(1)} collective-permute-done((f32[1024,32]{0,1:T(8,128)S(1)}, f32[1024,32]{0,1:T(8,128)S(1)}, u32[]{:S(2)}, u32[]{:S(2)}) %collective-permute-start.2) | collective-permute-done | bytes 131104 | tf_op jit(solution)/shard_map/ppermute | solution.py:12
  164.1 2.8 gather_fusion.7
  169.2 11.5 %all-gather.25.cloned.1.call-done = f32[1,1,1024,512]{3,2,1,0:T(8,128)} async-done(((f32[1,1,256,512]{3,2,1,0:T(8,128)}), f32[1,1,1024,512]{3,2,1,0:T(8,128)}) %all-gather.25.cloned.1.call-update) | async-done | bytes 2097168 | tf_op jit(solution)/shard_map/all_gather | solution.py:60
  180.7 2.9 fusion.31
  183.6 7.6 %collective-permute-start.3 = (f32[1024,32]{0,1:T(8,128)S(1)}, f32[1024,32]{0,1:T(8,128)S(1)}, u32[]{:S(2)}, u32[]{:S(2)}) collective-permute-start(f32[1024,32]{0,1:T(8,128)S(1)} %fusion.31), channel_id=1, source_target_pairs={{0,32},{4,36},{8,40},{12,44},{16,48},{20,52},{24,56},{28,60},{32,0... | collective-permute-start | bytes 393224 | tf_op jit(solution)/shard_map/ppermute | solution.py:12
  191.3 11.9 %collective-permute-done.3 = f32[1024,32]{0,1:T(8,128)S(1)} collective-permute-done((f32[1024,32]{0,1:T(8,128)S(1)}, f32[1024,32]{0,1:T(8,128)S(1)}, u32[]{:S(2)}, u32[]{:S(2)}) %collective-permute-start.3) | collective-permute-done | bytes 131104 | tf_op jit(solution)/shard_map/ppermute | solution.py:12
  203.5 2.8 gather_fusion.10
  208.6 12.7 %all-gather.27.cloned.1.call-done = f32[1,1,1024,512]{3,2,1,0:T(8,128)} async-done(((f32[1,1,256,512]{3,2,1,0:T(8,128)}), f32[1,1,1024,512]{3,2,1,0:T(8,128)}) %all-gather.27.cloned.1.call-update) | async-done | bytes 2097168 | tf_op jit(solution)/shard_map/all_gather | solution.py:60
  221.3 2.9 fusion.37
  224.2 12.8 %collective-permute-start.4 = (f32[1024,32]{0,1:T(8,128)S(1)}, f32[1024,32]{0,1:T(8,128)S(1)}, u32[]{:S(2)}, u32[]{:S(2)}) collective-permute-start(f32[1024,32]{0,1:T(8,128)S(1)} %fusion.37), channel_id=1, source_target_pairs={{0,64},{4,68},{8,72},{12,76},{16,80},{20,84},{24,88},{28,92},{32,9... | collective-permute-start | bytes 393224 | tf_op jit(solution)/shard_map/ppermute | solution.py:12
  237.0 3.7 %collective-permute-done.4 = f32[1024,32]{0,1:T(8,128)S(1)} collective-permute-done((f32[1024,32]{0,1:T(8,128)S(1)}, f32[1024,32]{0,1:T(8,128)S(1)}, u32[]{:S(2)}, u32[]{:S(2)}) %collective-permute-start.4) | collective-permute-done | bytes 131104 | tf_op jit(solution)/shard_map/ppermute | solution.py:12
  241.2 2.8 gather_fusion.13
  246.2 15.7 %all-gather.29.cloned.1.call-done = f32[1,1,1024,512]{3,2,1,0:T(8,128)} async-done(((f32[1,1,256,512]{3,2,1,0:T(8,128)}), f32[1,1,1024,512]{3,2,1,0:T(8,128)}) %all-gather.29.cloned.1.call-update) | async-done | bytes 2097168 | tf_op jit(solution)/shard_map/all_gather | solution.py:60
  261.9 2.9 fusion.43
  264.8 2.4 collective-permute-start.5
  267.3 4.6 %collective-permute-done.5 = f32[1024,32]{0,1:T(8,128)S(1)} collective-permute-done((f32[1024,32]{0,1:T(8,128)S(1)}, f32[1024,32]{0,1:T(8,128)S(1)}, u32[]{:S(2)}, u32[]{:S(2)}) %collective-permute-start.5) | collective-permute-done | bytes 131104 | tf_op jit(solution)/shard_map/ppermute | solution.py:12
  272.3 2.8 gather_fusion.16
  277.4 25.3 %all-gather.31.cloned.1.call-done = f32[1,1,1024,512]{3,2,1,0:T(8,128)} async-done(((f32[1,1,256,512]{3,2,1,0:T(8,128)}), f32[1,1,1024,512]{3,2,1,0:T(8,128)}) %all-gather.31.cloned.1.call-update) | async-done | bytes 2097168 | tf_op jit(solution)/shard_map/all_gather | solution.py:60
  302.7 2.9 fusion.49
  305.6 4.0 %collective-permute-start.6 = (f32[1024,32]{0,1:T(8,128)S(1)}, f32[1024,32]{0,1:T(8,128)S(1)}, u32[]{:S(2)}, u32[]{:S(2)}) collective-permute-start(f32[1024,32]{0,1:T(8,128)S(1)} %fusion.49), channel_id=1, source_target_pairs={{0,256},{4,260},{8,264},{12,268},{16,272},{20,276},{24,280},{28,28... | collective-permute-start | bytes 393224 | tf_op jit(solution)/shard_map/ppermute | solution.py:12
  310.5 3.3 all-to-all-start.2
  314.6 2.8 gather_fusion.19
  319.6 23.8 %all-gather.33.cloned.1.call-done = f32[1,1,1024,512]{3,2,1,0:T(8,128)} async-done(((f32[1,1,256,512]{3,2,1,0:T(8,128)}), f32[1,1,1024,512]{3,2,1,0:T(8,128)}) %all-gather.33.cloned.1.call-update) | async-done | bytes 2097168 | tf_op jit(solution)/shard_map/all_gather | solution.py:60
  343.5 2.9 fusion.58
  347.0 3.3 all-to-all-start.3
  351.1 5.2 %all-to-all-done.3 = f32[4,256,32]{1,2,0:T(8,128)S(1)} async-done(((f32[4,256,32]{1,2,0:T(8,128)}), f32[4,256,32]{1,2,0:T(8,128)S(1)}, u32[]{:S(2)}, u32[]{:S(2)}) %all-to-all-start.3) | async-done | bytes 131104 | tf_op jit(solution)/shard_map/all_to_all | solution.py:16
  (149 shorter events, 30.5 us)
Async XLA Ops:
  7.2 96.7 %all-gather.19.cloned.1.call-start = ((), (), s32[]{:S(2)}) async-start(), calls=%async_computation.4 | async-start | bytes 2621440 | tf_op jit(solution)/shard_map/all_gather | solution.py:28
  9.6 125.2 %all-gather.21.cloned.1.call-start = ((), (), s32[]{:S(2)}) async-start(), calls=%async_computation.5 | async-start | bytes 2621440 | tf_op jit(solution)/shard_map/all_gather | solution.py:60
  13.5 3.3 copy-start.1
  13.5 3.3 copy-start.2
  13.6 137.0 %all-gather.23.cloned.1.call-start = ((), (), s32[]{:S(2)}) async-start(), calls=%async_computation.6 | async-start | bytes 2621440 | tf_op jit(solution)/shard_map/all_gather | solution.py:60
  14.3 166.4 %all-gather.25.cloned.1.call-start = ((), (), s32[]{:S(2)}) async-start(), calls=%async_computation.7 | async-start | bytes 2621440 | tf_op jit(solution)/shard_map/all_gather | solution.py:60
  14.9 206.4 %all-gather.27.cloned.1.call-start = ((), (), s32[]{:S(2)}) async-start(), calls=%async_computation.8 | async-start | bytes 2621440 | tf_op jit(solution)/shard_map/all_gather | solution.py:60
  15.5 246.4 %all-gather.29.cloned.1.call-start = ((), (), s32[]{:S(2)}) async-start(), calls=%async_computation.9 | async-start | bytes 2621440 | tf_op jit(solution)/shard_map/all_gather | solution.py:60
  16.0 286.6 %all-gather.31.cloned.1.call-start = ((), (), s32[]{:S(2)}) async-start(), calls=%async_computation.10 | async-start | bytes 2621440 | tf_op jit(solution)/shard_map/all_gather | solution.py:60
  16.8 23.9 %copy-start.4 = (s32[1,32]{1,0:T(1,128)S(1)}, s32[1,32]{1,0:T(1,128)}, u32[]{:S(2)}) copy-start(s32[1,32]{1,0:T(1,128)} %param.15) | copy-start | bytes 388
  16.8 24.0 %copy-start.5 = (s32[1,32]{1,0:T(1,128)S(1)}, s32[1,32]{1,0:T(1,128)}, u32[]{:S(2)}) copy-start(s32[1,32]{1,0:T(1,128)} %param.14) | copy-start | bytes 388
  16.8 33.2 %copy-start.3 = (s32[1,7,2,1024]{3,2,1,0:T(2,128)S(1)}, s32[1,7,2,1024]{3,2,1,0:T(2,128)}, u32[]{:S(2)}) copy-start(s32[1,7,2,1024]{3,2,1,0:T(2,128)} %param.16) | copy-start | bytes 172036
  18.4 58.9 %all-to-all-start = ((f32[1,128,1280]{2,0,1:T(1,128)}), f32[1,128,1280]{2,0,1:T(1,128)S(1)}, u32[]{:S(2)}, u32[]{:S(2)}) async-start(f32[1,128,1280]{2,0,1:T(1,128)} %copy.232), calls=%async_computation | async-start | bytes 1310720 | tf_op jit(solution)/shard_map/all_to_all | solution.py:34
  38.0 305.4 %all-gather.33.cloned.1.call-start = ((), (), s32[]{:S(2)}) async-start(), calls=%async_computation.11 | async-start | bytes 2621440 | tf_op jit(solution)/shard_map/all_gather | solution.py:60
  78.2 22.6 %all-to-all-start.1 = ((f32[4,32,1280]{2,1,0:T(8,128)}), f32[4,32,1280]{2,1,0:T(8,128)S(1)}, u32[]{:S(2)}, u32[]{:S(2)}) async-start(f32[4,32,1280]{2,1,0:T(8,128)} %bitcast.67), calls=%async_computation.1 | async-start | bytes 1310720 | tf_op jit(solution)/shard_map/all_to_all | solution.py:35
  122.1 3.6 %copy-start = (f32[32,4,256]{0,2,1:T(8,128)S(1)}, f32[32,4,256]{0,2,1:T(8,128)}, u32[]{:S(2)}) copy-start(f32[32,4,256]{0,2,1:T(8,128)} %copy.233) | copy-start | bytes 393220
  125.8 3.8 %collective-permute-start = (f32[1024,32]{1,0:T(8,128)S(1)}, f32[1024,32]{1,0:T(8,128)S(1)}, u32[]{:S(2)}, u32[]{:S(2)}) collective-permute-start(f32[1024,32]{1,0:T(8,128)S(1)} %bitcast_subtract_fusion), channel_id=1, source_target_pairs={{0,4},{4,0},{8,12},{12,8},{16,20},{20,16},{24,28},{28,24},{32,36},... | collective-permute-start | bytes 393224 | tf_op jit(solution)/shard_map/ppermute | solution.py:12
  137.8 7.4 %collective-permute-start.1 = (f32[1024,32]{0,1:T(8,128)S(1)}, f32[1024,32]{0,1:T(8,128)S(1)}, u32[]{:S(2)}, u32[]{:S(2)}) collective-permute-start(f32[1024,32]{0,1:T(8,128)S(1)} %select_subtract_fusion), channel_id=1, source_target_pairs={{0,8},{4,12},{8,0},{12,4},{16,24},{20,28},{24,16},{28,20},{32,40},... | collective-permute-start | bytes 393224 | tf_op jit(solution)/shard_map/ppermute | solution.py:12
  153.5 10.3 %collective-permute-start.2 = (f32[1024,32]{0,1:T(8,128)S(1)}, f32[1024,32]{0,1:T(8,128)S(1)}, u32[]{:S(2)}, u32[]{:S(2)}) collective-permute-start(f32[1024,32]{0,1:T(8,128)S(1)} %fusion.25), channel_id=1, source_target_pairs={{0,16},{4,20},{8,24},{12,28},{16,0},{20,4},{24,8},{28,12},{32,48},... | collective-permute-start | bytes 393224 | tf_op jit(solution)/shard_map/ppermute | solution.py:12
  183.6 19.6 %collective-permute-start.3 = (f32[1024,32]{0,1:T(8,128)S(1)}, f32[1024,32]{0,1:T(8,128)S(1)}, u32[]{:S(2)}, u32[]{:S(2)}) collective-permute-start(f32[1024,32]{0,1:T(8,128)S(1)} %fusion.31), channel_id=1, source_target_pairs={{0,32},{4,36},{8,40},{12,44},{16,48},{20,52},{24,56},{28,60},{32,0... | collective-permute-start | bytes 393224 | tf_op jit(solution)/shard_map/ppermute | solution.py:12
  224.2 16.6 %collective-permute-start.4 = (f32[1024,32]{0,1:T(8,128)S(1)}, f32[1024,32]{0,1:T(8,128)S(1)}, u32[]{:S(2)}, u32[]{:S(2)}) collective-permute-start(f32[1024,32]{0,1:T(8,128)S(1)} %fusion.37), channel_id=1, source_target_pairs={{0,64},{4,68},{8,72},{12,76},{16,80},{20,84},{24,88},{28,92},{32,9... | collective-permute-start | bytes 393224 | tf_op jit(solution)/shard_map/ppermute | solution.py:12
  264.8 7.1 %collective-permute-start.5 = (f32[1024,32]{0,1:T(8,128)S(1)}, f32[1024,32]{0,1:T(8,128)S(1)}, u32[]{:S(2)}, u32[]{:S(2)}) collective-permute-start(f32[1024,32]{0,1:T(8,128)S(1)} %fusion.43), channel_id=1, source_target_pairs={{0,128},{4,132},{8,136},{12,140},{16,144},{20,148},{24,152},{28,15... | collective-permute-start | bytes 393224 | tf_op jit(solution)/shard_map/ppermute | solution.py:12
  305.6 8.6 %collective-permute-start.6 = (f32[1024,32]{0,1:T(8,128)S(1)}, f32[1024,32]{0,1:T(8,128)S(1)}, u32[]{:S(2)}, u32[]{:S(2)}) collective-permute-start(f32[1024,32]{0,1:T(8,128)S(1)} %fusion.49), channel_id=1, source_target_pairs={{0,256},{4,260},{8,264},{12,268},{16,272},{20,276},{24,280},{28,28... | collective-permute-start | bytes 393224 | tf_op jit(solution)/shard_map/ppermute | solution.py:12
  310.5 36.5 %all-to-all-start.2 = ((f32[4,256,32]{1,2,0:T(8,128)}), f32[4,256,32]{1,2,0:T(8,128)S(1)}, u32[]{:S(2)}, u32[]{:S(2)}) async-start(f32[4,256,32]{1,2,0:T(8,128)} %copy.240), calls=%async_computation.2 | async-start | bytes 262144 | tf_op jit(solution)/shard_map/all_to_all | solution.py:16
  347.0 9.3 %all-to-all-start.3 = ((f32[4,256,32]{1,2,0:T(8,128)}), f32[4,256,32]{1,2,0:T(8,128)S(1)}, u32[]{:S(2)}, u32[]{:S(2)}) async-start(f32[4,256,32]{1,2,0:T(8,128)} %bitcast.157), calls=%async_computation.3 | async-start | bytes 262144 | tf_op jit(solution)/shard_map/all_to_all | solution.py:16
Sparse Core Ops, SparseCore 0:
  10.1 42.9 all-gather.18
  55.2 45.4 all-gather.20
  102.8 37.2 all-gather.22
  142.1 38.5 all-gather.24
  182.7 38.5 all-gather.26
  223.2 38.5 all-gather.28
  264.0 38.6 all-gather.30
  304.8 38.6 all-gather.32
where the time goes:
time: 365 us; the launch traced here: 364 us
  waiting for transfers between devices  177 us (48%)
  local copies, waits for them, and re-layouts  68 us (19%)
  starting transfers between devices  65.1 us (18%)
  matrix products  27.6 us (8%)
  between operations  16.1 us (4%)
  blocking collectives  9.04 us (2%)
    all_gather x7, waiting for transfers between devices, on_device(): lax.all_gather(merge_maps[0, level - 1], 'case', axis=0, tiled=True)  89 us
    ppermute x7, waiting for transfers between devices, from_partner(): return lax.ppermute(value, axis, pairs)  34.6 us
    ppermute x7, starting transfers between devices, from_partner(): return lax.ppermute(value, axis, pairs)  34.3 us
    all_to_all x1, waiting for transfers between devices, on_device(): lax.all_to_all(joined, 'sub', split_axis=1, concat_axis=0, tiled=True)  26.4 us
    gather x14, local copies, waits for them, and re-layouts, on_device(): jnp.take(stacked, kept_index, axis=0)  20.9 us
    dot_general x7, matrix products, on_device(): jnp.dot(matrix, shared, precision=lax.Precision.HIGH)  20.2 us
    all_to_all x1, starting transfers between devices, on_device(): lax.all_to_all(joined, 'sub', split_axis=1, concat_axis=0, tiled=True)  19.6 us
    all_to_all x1, waiting for transfers between devices, on_device(): lax.all_to_all(joined, 'case', split_axis=0, concat_axis=1, tiled=True)  18.3 us
  transfers between devices with their start and end apart: 19, of which 15 were waited for; matrix products, arithmetic and copies ran while one was open for 26% of the time, Pallas kernels for 0%

commit v1 on v0

--- a/solution.py
+++ b/solution.py
@@ -57,7 +57,12 @@
     for level in range(1, levels + 1):
         half = 1 << level - 1
         maps = interface_maps[0, level - 1]
-        matrix = lax.all_gather(merge_maps[0, level - 1], "case", axis=0, tiled=True)
+        matrix = jnp.concatenate(
+            lax.all_to_all(
+                jnp.stack([merge_maps[0, level - 1]] * lax.axis_size("case")), "case", 0, 0
+            ),
+            axis=0,
+        )
         shared_rows = matrix.shape[1]
         upper = slot // half % 2 == 1
         other = from_partner(current, "sub", level - 1)

time: 365 us -> 424 us (1.16)
  waiting for transfers between devices: 177 us -> 125 us
  local copies, waits for them, and re-layouts: 68 us -> 101 us
  blocking collectives: 9.04 us -> 37.8 us
  other arithmetic: 0.76 us -> 27.3 us
  starting transfers between devices: 65.1 us -> 88.8 us
    all_gather x7 -> x0, waiting for transfers between devices: 89 us -> none  [on_device(): lax.all_gather(merge_maps[0, level - 1], 'case', axis=0, tiled=True)]
    all_to_all x0 -> x7, waiting for transfers between devices: none -> 39.4 us  [on_device(): lax.all_to_all(jnp.stack([merge_maps[0, level - 1]] * lax.axis_size('case...]
    all_to_all x0 -> x7, starting transfers between devices: none -> 30.6 us  [on_device(): lax.all_to_all(jnp.stack([merge_maps[0, level - 1]] * lax.axis_size('case...]
    all_gather x1, blocking collectives: 9.04 us -> 37.8 us  [on_device(): cols_of_blocks = lax.all_gather(block_cols[0], 'case', axis=0, tiled=True)]
    another operation x0 -> x8, local copies, waits for them, and re-layouts: none -> 17.2 us  [on_device(): jnp.stack([merge_maps[0, level - 1]] * lax.axis_size('case'))]
    gather x14, local copies, waits for them, and re-layouts: 20.9 us -> 31.5 us  [on_device(): jnp.take(stacked, kept_index, axis=0)]
    all_to_all x1, waiting for transfers between devices: 18.3 us -> 8.22 us  [on_device(): lax.all_to_all(joined, 'case', split_axis=0, concat_axis=1, tiled=True)]
    gather x21, other arithmetic: 0.16 us -> 10.2 us
  transfers between devices with their start and end apart: 19 -> 19, of which waited for: 15 -> 11; matrix products, arithmetic and copies ran while one was open for 26% -> 36% of each run, Pallas kernels for 0% -> 0%
where the time goes in v1:
time: 424 us; the launch traced here: 422 us
  waiting for transfers between devices  125 us (29%)
  local copies, waits for them, and re-layouts  101 us (24%)
  starting transfers between devices  88.8 us (21%)
  blocking collectives  37.8 us (9%)
  other arithmetic  27.3 us (6%)
  matrix products  26.6 us (6%)
  between operations  15.6 us (4%)
    all_to_all x7, waiting for transfers between devices, on_device(): lax.all_to_all(jnp.stack([merge_maps[0, level - 1]] * lax.axis_size('case...  39.4 us
    all_gather x1, blocking collectives, on_device(): cols_of_blocks = lax.all_gather(block_cols[0], 'case', axis=0, tiled=True)  37.8 us
    ppermute x7, waiting for transfers between devices, from_partner(): return lax.ppermute(value, axis, pairs)  34.7 us
    all_to_all x1, waiting for transfers between devices, on_device(): lax.all_to_all(joined, 'sub', split_axis=1, concat_axis=0, tiled=True)  34.6 us
    gather x14, local copies, waits for them, and re-layouts, on_device(): jnp.take(stacked, kept_index, axis=0)  31.5 us
    all_to_all x7, starting transfers between devices, on_device(): lax.all_to_all(jnp.stack([merge_maps[0, level - 1]] * lax.axis_size('case...  30.6 us
    ppermute x7, starting transfers between devices, from_partner(): return lax.ppermute(value, axis, pairs)  24.3 us
    all_to_all x1, starting transfers between devices, on_device(): lax.all_to_all(joined, 'sub', split_axis=1, concat_axis=0, tiled=True)  22.6 us
  transfers between devices with their start and end apart: 19, of which 11 were waited for; matrix products, arithmetic and copies ran while one was open for 36% of the time, Pallas kernels for 0%

profile of v1, /device:TPU:8, one launch (start us, length us, event | category | flops | bytes accessed | tf_op | source)
XLA Modules:
  0.0 421.8 jit_solution(9002813800673230125)
XLA Ops:
  9.6 3.5 slice_bitcast_fusion.7
  14.8 4.4 %all-to-all-start.3 = ((f32[4,256,512]{2,1,0:T(8,128)}), f32[4,256,512]{2,1,0:T(8,128)S(1)}, u32[]{:S(2)}, u32[]{:S(2)}) async-start(f32[4,256,512]{2,1,0:T(8,128)} %stack.21), calls=%async_computation.3 | async-start | bytes 4194304 | tf_op jit(solution)/shard_map/all_to_all | solution.py:61
  21.4 37.8 %all-reduce.2 = (s32[128]{0:T(128)S(1)}, s32[128]{0:T(128)S(1)}) all-reduce(s32[128]{0:T(128)S(1)} %bitcast_dynamic-update-slice_fusion, s32[128]{0:T(128)S(1)} %bitcast_dynamic-update-slice_fusion.1), channel_id=3, replica_groups=mesh['sub'=128,'case'=4] {'case'}, use_global_device_ids=true, to_apply=%add.1 | all-reduce | flops 256 | bytes 2048 | tf_op jit(solution)/shard_map/all_gather | solution.py:30
  65.8 3.0 stack.22
  68.8 4.5 %all-to-all-start.4 = ((f32[4,256,512]{2,1,0:T(8,128)}), f32[4,256,512]{2,1,0:T(8,128)}, u32[]{:S(2)}, u32[]{:S(2)}) async-start(f32[4,256,512]{2,1,0:T(8,128)} %stack.22), calls=%async_computation.4 | async-start | bytes 4194304 | tf_op jit(solution)/shard_map/all_to_all | solution.py:61
  77.3 17.9 %all-to-all-done.4 = f32[4,256,512]{2,1,0:T(8,128)} async-done(((f32[4,256,512]{2,1,0:T(8,128)}), f32[4,256,512]{2,1,0:T(8,128)}, u32[]{:S(2)}, u32[]{:S(2)}) %all-to-all-start.4) | async-done | bytes 2097184 | tf_op jit(solution)/shard_map/all_to_all | solution.py:61
  95.3 22.6 %all-to-all-start = ((f32[1,128,1280]{2,0,1:T(1,128)}), f32[1,128,1280]{2,0,1:T(1,128)S(1)}, u32[]{:S(2)}, u32[]{:S(2)}) async-start(f32[1,128,1280]{2,0,1:T(1,128)} %copy.232), calls=%async_computation | async-start | bytes 1310720 | tf_op jit(solution)/shard_map/all_to_all | solution.py:34
  122.6 34.6 %all-to-all-done = f32[1,128,1280]{2,0,1:T(1,128)S(1)} async-done(((f32[1,128,1280]{2,0,1:T(1,128)}), f32[1,128,1280]{2,0,1:T(1,128)S(1)}, u32[]{:S(2)}, u32[]{:S(2)}) %all-to-all-start) | async-done | bytes 655392 | tf_op jit(solution)/shard_map/all_to_all | solution.py:34
  157.2 2.7 stack.23
  159.8 3.6 all-to-all-start.5
  167.7 21.5 %all-to-all-done.5 = f32[4,256,512]{2,1,0:T(8,128)S(1)} async-done(((f32[4,256,512]{2,1,0:T(8,128)}), f32[4,256,512]{2,1,0:T(8,128)S(1)}, u32[]{:S(2)}, u32[]{:S(2)}) %all-to-all-start.5) | async-done | bytes 2097184 | tf_op jit(solution)/shard_map/all_to_all | solution.py:61
  189.2 3.5 all-to-all-start.1
  193.9 8.2 %all-to-all-done.1 = f32[4,32,1280]{2,1,0:T(8,128)S(1)} async-done(((f32[4,32,1280]{2,1,0:T(8,128)}), f32[4,32,1280]{2,1,0:T(8,128)S(1)}, u32[]{:S(2)}, u32[]{:S(2)}) %all-to-all-start.1) | async-done | bytes 655392 | tf_op jit(solution)/shard_map/all_to_all | solution.py:35
  203.7 4.6 %all-to-all-start.6 = ((f32[4,256,512]{2,1,0:T(8,128)}), f32[4,256,512]{2,1,0:T(8,128)}, u32[]{:S(2)}, u32[]{:S(2)}) async-start(f32[4,256,512]{2,1,0:T(8,128)} %stack.24), calls=%async_computation.6 | async-start | bytes 4194304 | tf_op jit(solution)/shard_map/all_to_all | solution.py:61
  212.5 5.6 %copy.237 = f32[1,128,4096]{1,2,0:T(8,128)} copy(f32[1,128,4096]{2,0,1:T(1,128)} %all-gather.5.cloned.1.call-done) | data formatting | bytes 4194304 | tf_op jit(solution)/shard_map/all_gather | solution.py:28
  218.1 5.6 %copy.238 = f32[128,64,64]{2,1,0:T(8,128)} copy(f32[128,64,64]{0,2,1:T(8,128)} %bitcast.135) | data formatting | bytes 4194304 | tf_op jit(solution)/shard_map/reshape | solution.py:32
  223.8 6.9 %fusion.2 = f32[128,64,32]{1,2,0:T(8,128)} fusion(f32[128,64,64]{2,1,0:T(8,128)} %copy.238, f32[128,64,32]{1,2,0:T(8,128)S(1)} %gather_fusion, pred[128]{0:T(512)(128)(4,1)S(1)} %compare_and_fusion.21), kind=kOutput, calls=%fused_computation.24 | convolution fusion | flops 100925440 | bytes 4194432 | tf_op jit(solution)/shard_map/krc,kcn->krn/dot_general | solution.py:43
  230.7 3.1 copy.239
  238.0 4.6 %all-to-all-start.7 = ((f32[4,256,512]{2,1,0:T(8,128)}), f32[4,256,512]{2,1,0:T(8,128)}, u32[]{:S(2)}, u32[]{:S(2)}) async-start(f32[4,256,512]{2,1,0:T(8,128)} %stack.25), calls=%async_computation.7 | async-start | bytes 4194304 | tf_op jit(solution)/shard_map/all_to_all | solution.py:61
  243.9 2.8 gather_fusion.1
  252.6 3.0 collective-permute-start.1
  255.7 4.6 %collective-permute-done.1 = f32[1024,32]{0,1:T(8,128)S(1)} collective-permute-done((f32[1024,32]{0,1:T(8,128)S(1)}, f32[1024,32]{0,1:T(8,128)S(1)}, u32[]{:S(2)}, u32[]{:S(2)}) %collective-permute-start.1) | collective-permute-done | bytes 131104 | tf_op jit(solution)/shard_map/ppermute | solution.py:12
  260.6 2.8 gather_fusion.4
  265.8 2.9 fusion.11
  268.7 3.3 collective-permute-start.2
  274.2 4.6 %all-to-all-start.8 = ((f32[4,256,512]{2,1,0:T(8,128)}), f32[4,256,512]{2,1,0:T(8,128)}, u32[]{:S(2)}, u32[]{:S(2)}) async-start(f32[4,256,512]{2,1,0:T(8,128)} %stack.26), calls=%async_computation.8 | async-start | bytes 4194304 | tf_op jit(solution)/shard_map/all_to_all | solution.py:61
  279.7 2.8 gather_fusion.7
  289.1 3.4 collective-permute-start.3
  293.1 14.9 %collective-permute-done.3 = f32[1024,32]{0,1:T(8,128)S(1)} collective-permute-done((f32[1024,32]{0,1:T(8,128)S(1)}, f32[1024,32]{0,1:T(8,128)S(1)}, u32[]{:S(2)}, u32[]{:S(2)}) %collective-permute-start.3) | collective-permute-done | bytes 131104 | tf_op jit(solution)/shard_map/ppermute | solution.py:12
  308.3 2.8 gather_fusion.10
  313.5 2.9 fusion.9
  316.4 6.2 %collective-permute-start.4 = (f32[1024,32]{0,1:T(8,128)S(1)}, f32[1024,32]{0,1:T(8,128)S(1)}, u32[]{:S(2)}, u32[]{:S(2)}) collective-permute-start(f32[1024,32]{0,1:T(8,128)S(1)} %fusion.9), channel_id=1, source_target_pairs={{0,64},{4,68},{8,72},{12,76},{16,80},{20,84},{24,88},{28,92},{32,9... | collective-permute-start | bytes 393224 | tf_op jit(solution)/shard_map/ppermute | solution.py:12
  325.3 4.3 %all-to-all-start.9 = ((f32[4,256,512]{2,1,0:T(8,128)}), f32[4,256,512]{2,1,0:T(8,128)S(1)}, u32[]{:S(2)}, u32[]{:S(2)}) async-start(f32[4,256,512]{2,1,0:T(8,128)} %stack.27), calls=%async_computation.9 | async-start | bytes 4194304 | tf_op jit(solution)/shard_map/all_to_all | solution.py:61
  329.7 8.2 %collective-permute-done.4 = f32[1024,32]{0,1:T(8,128)S(1)} collective-permute-done((f32[1024,32]{0,1:T(8,128)S(1)}, f32[1024,32]{0,1:T(8,128)S(1)}, u32[]{:S(2)}, u32[]{:S(2)}) %collective-permute-start.4) | collective-permute-done | bytes 131104 | tf_op jit(solution)/shard_map/ppermute | solution.py:12
  339.9 4.3 %gather_fusion.13 = f32[1024,32]{1,0:T(8,128)} fusion(f32[2048,32]{1,0:T(8,128)S(1)} %copy.254, s32[1024]{0:T(1024)} %fusion.48), kind=kCustom, calls=%fused_computation.5.clone | custom fusion | bytes 266240 | tf_op jit(solution)/shard_map/jit(_take)/gather | solution.py:83
  349.7 3.1 fusion.8
  352.8 3.1 collective-permute-start.5
  356.5 3.6 collective-permute-done.5
  362.2 4.3 %gather_fusion.16 = f32[1024,32]{1,0:T(8,128)} fusion(f32[2048,32]{1,0:T(8,128)S(1)} %copy.258, s32[1024]{0:T(1024)} %fusion.49), kind=kCustom, calls=%fused_computation.6.clone | custom fusion | bytes 266240 | tf_op jit(solution)/shard_map/jit(_take)/gather | solution.py:83
  371.8 3.2 fusion.7
  375.0 3.5 collective-permute-start.6
  379.9 3.4 collective-permute-done.6
  385.4 4.0 gather_fusion.19
  394.5 4.5 %all-to-all-start.2 = ((f32[4,256,32]{1,2,0:T(8,128)}), f32[4,256,32]{1,2,0:T(8,128)S(1)}, u32[]{:S(2)}, u32[]{:S(2)}) async-start(f32[4,256,32]{1,2,0:T(8,128)} %copy.240), calls=%async_computation.2 | async-start | bytes 262144 | tf_op jit(solution)/shard_map/all_to_all | solution.py:16
  399.0 2.4 fusion.6
  402.1 2.9 all-to-all-done.2
  404.9 3.3 all-to-all-start.10
  409.0 5.2 %all-to-all-done.10 = f32[4,256,32]{1,2,0:T(8,128)S(1)} async-done(((f32[4,256,32]{1,2,0:T(8,128)}), f32[4,256,32]{1,2,0:T(8,128)S(1)}, u32[]{:S(2)}, u32[]{:S(2)}) %all-to-all-start.10) | async-done | bytes 131104 | tf_op jit(solution)/shard_map/all_to_all | solution.py:16
  (231 shorter events, 87.7 us)
Async XLA Ops:
  7.2 205.3 %all-gather.5.cloned.1.call-start = ((), (), s32[]{:S(2)}) async-start(), calls=%async_computation.11 | async-start | bytes 2621440 | tf_op jit(solution)/shard_map/all_gather | solution.py:28
  14.8 6.4 %copy-start.45 = (s32[1,32]{1,0:T(1,128)S(1)}, s32[1,32]{1,0:T(1,128)}, u32[]{:S(2)}) copy-start(s32[1,32]{1,0:T(1,128)} %param.15) | copy-start | bytes 388
  14.8 6.5 %copy-start.46 = (s32[1,32]{1,0:T(1,128)S(1)}, s32[1,32]{1,0:T(1,128)}, u32[]{:S(2)}) copy-start(s32[1,32]{1,0:T(1,128)} %param.14) | copy-start | bytes 388
  14.8 44.4 %copy-start.13 = (f32[1,128,256]{2,1,0:T(8,128)S(1)}, f32[1,128,256]{2,1,0:T(8,128)}, u32[]{:S(2)}) copy-start(f32[1,128,256]{2,1,0:T(8,128)} %param.12) | copy-start | bytes 393220
  14.8 51.0 %all-to-all-start.3 = ((f32[4,256,512]{2,1,0:T(8,128)}), f32[4,256,512]{2,1,0:T(8,128)S(1)}, u32[]{:S(2)}, u32[]{:S(2)}) async-start(f32[4,256,512]{2,1,0:T(8,128)} %stack.21), calls=%async_computation.3 | async-start | bytes 4194304 | tf_op jit(solution)/shard_map/all_to_all | solution.py:61
  68.8 26.5 %all-to-all-start.4 = ((f32[4,256,512]{2,1,0:T(8,128)}), f32[4,256,512]{2,1,0:T(8,128)}, u32[]{:S(2)}, u32[]{:S(2)}) async-start(f32[4,256,512]{2,1,0:T(8,128)} %stack.22), calls=%async_computation.4 | async-start | bytes 4194304 | tf_op jit(solution)/shard_map/all_to_all | solution.py:61
  95.3 61.9 %all-to-all-start = ((f32[1,128,1280]{2,0,1:T(1,128)}), f32[1,128,1280]{2,0,1:T(1,128)S(1)}, u32[]{:S(2)}, u32[]{:S(2)}) async-start(f32[1,128,1280]{2,0,1:T(1,128)} %copy.232), calls=%async_computation | async-start | bytes 1310720 | tf_op jit(solution)/shard_map/all_to_all | solution.py:34
  120.8 122.3 %copy-start.21 = (s32[512]{0:T(512)}, s32[512]{0:T(512)S(1)}, u32[]{:S(2)}) copy-start(s32[512]{0:T(512)S(1)} %add_select_fusion.22) | copy-start | bytes 6148
  120.9 122.3 %copy-start.23 = (s32[512]{0:T(512)}, s32[512]{0:T(512)S(1)}, u32[]{:S(2)}) copy-start(s32[512]{0:T(512)S(1)} %add_select_fusion.23) | copy-start | bytes 6148
  159.8 29.4 %all-to-all-start.5 = ((f32[4,256,512]{2,1,0:T(8,128)}), f32[4,256,512]{2,1,0:T(8,128)S(1)}, u32[]{:S(2)}, u32[]{:S(2)}) async-start(f32[4,256,512]{2,1,0:T(8,128)} %stack.23), calls=%async_computation.5 | async-start | bytes 4194304 | tf_op jit(solution)/shard_map/all_to_all | solution.py:61
  189.2 14.5 %copy-start.2 = (f32[4,256,512]{2,1,0:T(8,128)}, f32[4,256,512]{2,1,0:T(8,128)S(1)}, u32[]{:S(2)}) copy-start(f32[4,256,512]{2,1,0:T(8,128)S(1)} %all-to-all-done.5) | copy-start | bytes 6291460
  189.2 12.9 %all-to-all-start.1 = ((f32[4,32,1280]{2,1,0:T(8,128)}), f32[4,32,1280]{2,1,0:T(8,128)S(1)}, u32[]{:S(2)}, u32[]{:S(2)}) async-start(f32[4,32,1280]{2,1,0:T(8,128)} %bitcast.74), calls=%async_computation.1 | async-start | bytes 1310720 | tf_op jit(solution)/shard_map/all_to_all | solution.py:35
  203.7 32.7 %all-to-all-start.6 = ((f32[4,256,512]{2,1,0:T(8,128)}), f32[4,256,512]{2,1,0:T(8,128)}, u32[]{:S(2)}, u32[]{:S(2)}) async-start(f32[4,256,512]{2,1,0:T(8,128)} %stack.24), calls=%async_computation.6 | async-start | bytes 4194304 | tf_op jit(solution)/shard_map/all_to_all | solution.py:61
  234.4 9.3 %copy-start.4 = (f32[1024,32]{1,0:T(8,128)}, f32[1024,32]{1,0:T(8,128)S(1)}, u32[]{:S(2)}) copy-start(f32[1024,32]{1,0:T(8,128)S(1)} %bitcast_subtract_fusion) | copy-start | bytes 393220
  234.4 9.3 %collective-permute-start = (f32[1024,32]{1,0:T(8,128)S(1)}, f32[1024,32]{1,0:T(8,128)S(1)}, u32[]{:S(2)}, u32[]{:S(2)}) collective-permute-start(f32[1024,32]{1,0:T(8,128)S(1)} %bitcast_subtract_fusion), channel_id=1, source_target_pairs={{0,4},{4,0},{8,12},{12,8},{16,20},{20,16},{24,28},{28,24},{32,36},... | collective-permute-start | bytes 393224 | tf_op jit(solution)/shard_map/ppermute | solution.py:12
  238.0 34.6 %all-to-all-start.7 = ((f32[4,256,512]{2,1,0:T(8,128)}), f32[4,256,512]{2,1,0:T(8,128)}, u32[]{:S(2)}, u32[]{:S(2)}) async-start(f32[4,256,512]{2,1,0:T(8,128)} %stack.25), calls=%async_computation.7 | async-start | bytes 4194304 | tf_op jit(solution)/shard_map/all_to_all | solution.py:61
  250.2 5.4 %copy-start.22 = (s32[512]{0:T(512)S(1)}, s32[512]{0:T(512)}, u32[]{:S(2)}) copy-start(s32[512]{0:T(512)} %copy-done.21) | copy-start | bytes 6148
  250.2 5.4 %copy-start.24 = (s32[512]{0:T(512)S(1)}, s32[512]{0:T(512)}, u32[]{:S(2)}) copy-start(s32[512]{0:T(512)} %copy-done.23) | copy-start | bytes 6148
  250.2 5.4 %copy-start.17 = (s32[512]{0:T(512)S(1)}, s32[512]{0:T(512)}, u32[]{:S(2)}) copy-start(s32[512]{0:T(512)} %add_select_fusion.18) | copy-start | bytes 6148
  250.2 5.4 %copy-start.18 = (s32[512]{0:T(512)S(1)}, s32[512]{0:T(512)}, u32[]{:S(2)}) copy-start(s32[512]{0:T(512)} %add_select_fusion.19) | copy-start | bytes 6148
  250.2 10.4 %copy-start.26 = (s32[1024]{0:T(1024)S(1)}, s32[1024]{0:T(1024)}, u32[]{:S(2)}) copy-start(s32[1024]{0:T(1024)} %fusion.45) | copy-start | bytes 12292
  252.6 7.7 %collective-permute-start.1 = (f32[1024,32]{0,1:T(8,128)S(1)}, f32[1024,32]{0,1:T(8,128)S(1)}, u32[]{:S(2)}, u32[]{:S(2)}) collective-permute-start(f32[1024,32]{0,1:T(8,128)S(1)} %select_subtract_fusion), channel_id=1, source_target_pairs={{0,8},{4,12},{8,0},{12,4},{16,24},{20,28},{24,16},{28,20},{32,40},... | collective-permute-start | bytes 393224 | tf_op jit(solution)/shard_map/ppermute | solution.py:12
  264.7 7.9 %copy-start.7 = (f32[256,512]{1,0:T(8,128)S(1)}, f32[256,512]{1,0:T(8,128)}, u32[]{:S(2)}) copy-start(f32[256,512]{1,0:T(8,128)} %get-tuple-element.52) | copy-start | bytes 1572868
  268.7 10.7 %collective-permute-start.2 = (f32[1024,32]{0,1:T(8,128)S(1)}, f32[1024,32]{0,1:T(8,128)S(1)}, u32[]{:S(2)}, u32[]{:S(2)}) collective-permute-start(f32[1024,32]{0,1:T(8,128)S(1)} %fusion.11), channel_id=1, source_target_pairs={{0,16},{4,20},{8,24},{12,28},{16,0},{20,4},{24,8},{28,12},{32,48},... | collective-permute-start | bytes 393224 | tf_op jit(solution)/shard_map/ppermute | solution.py:12
  274.2 49.5 %all-to-all-start.8 = ((f32[4,256,512]{2,1,0:T(8,128)}), f32[4,256,512]{2,1,0:T(8,128)}, u32[]{:S(2)}, u32[]{:S(2)}) async-start(f32[4,256,512]{2,1,0:T(8,128)} %stack.26), calls=%async_computation.8 | async-start | bytes 4194304 | tf_op jit(solution)/shard_map/all_to_all | solution.py:61
  286.7 5.8 %copy-start.19 = (s32[512]{0:T(512)S(1)}, s32[512]{0:T(512)}, u32[]{:S(2)}) copy-start(s32[512]{0:T(512)} %add_select_fusion.10) | copy-start | bytes 6148
  286.7 5.8 %copy-start.20 = (s32[512]{0:T(512)S(1)}, s32[512]{0:T(512)}, u32[]{:S(2)}) copy-start(s32[512]{0:T(512)} %add_select_fusion.11) | copy-start | bytes 6148
  286.7 21.6 %copy-start.25 = (s32[1024]{0:T(1024)S(1)}, s32[1024]{0:T(1024)}, u32[]{:S(2)}) copy-start(s32[1024]{0:T(1024)} %fusion.47) | copy-start | bytes 12292
  289.1 18.9 %collective-permute-start.3 = (f32[1024,32]{0,1:T(8,128)S(1)}, f32[1024,32]{0,1:T(8,128)S(1)}, u32[]{:S(2)}, u32[]{:S(2)}) collective-permute-start(f32[1024,32]{0,1:T(8,128)S(1)} %fusion.10), channel_id=1, source_target_pairs={{0,32},{4,36},{8,40},{12,44},{16,48},{20,52},{24,56},{28,60},{32,0... | collective-permute-start | bytes 393224 | tf_op jit(solution)/shard_map/ppermute | solution.py:12
  312.4 10.7 %copy-start.15 = (s32[512]{0:T(512)S(1)}, s32[512]{0:T(512)}, u32[]{:S(2)}) copy-start(s32[512]{0:T(512)} %add_select_fusion.6) | copy-start | bytes 6148
  312.4 10.7 %copy-start.16 = (s32[512]{0:T(512)S(1)}, s32[512]{0:T(512)}, u32[]{:S(2)}) copy-start(s32[512]{0:T(512)} %add_select_fusion.7) | copy-start | bytes 6148
  312.4 11.3 %copy-start.6 = (f32[256,512]{1,0:T(8,128)S(1)}, f32[256,512]{1,0:T(8,128)}, u32[]{:S(2)}) copy-start(f32[256,512]{1,0:T(8,128)} %get-tuple-element.51) | copy-start | bytes 1572868
  316.4 21.5 %copy-start.10 = (f32[1024,32]{0,1:T(8,128)}, f32[1024,32]{0,1:T(8,128)S(1)}, u32[]{:S(2)}) copy-start(f32[1024,32]{0,1:T(8,128)S(1)} %fusion.9) | copy-start | bytes 393220
  316.4 21.4 %collective-permute-start.4 = (f32[1024,32]{0,1:T(8,128)S(1)}, f32[1024,32]{0,1:T(8,128)S(1)}, u32[]{:S(2)}, u32[]{:S(2)}) collective-permute-start(f32[1024,32]{0,1:T(8,128)S(1)} %fusion.9), channel_id=1, source_target_pairs={{0,64},{4,68},{8,72},{12,76},{16,80},{20,84},{24,88},{28,92},{32,9... | collective-permute-start | bytes 393224 | tf_op jit(solution)/shard_map/ppermute | solution.py:12
  325.3 69.2 %all-to-all-start.9 = ((f32[4,256,512]{2,1,0:T(8,128)}), f32[4,256,512]{2,1,0:T(8,128)S(1)}, u32[]{:S(2)}, u32[]{:S(2)}) async-start(f32[4,256,512]{2,1,0:T(8,128)} %stack.27), calls=%async_computation.9 | async-start | bytes 4194304 | tf_op jit(solution)/shard_map/all_to_all | solution.py:61
  352.8 7.3 %copy-start.11 = (f32[1024,32]{0,1:T(8,128)}, f32[1024,32]{0,1:T(8,128)S(1)}, u32[]{:S(2)}) copy-start(f32[1024,32]{0,1:T(8,128)S(1)} %fusion.8) | copy-start | bytes 393220
  352.8 7.3 %collective-permute-start.5 = (f32[1024,32]{0,1:T(8,128)S(1)}, f32[1024,32]{0,1:T(8,128)S(1)}, u32[]{:S(2)}, u32[]{:S(2)}) collective-permute-start(f32[1024,32]{0,1:T(8,128)S(1)} %fusion.8), channel_id=1, source_target_pairs={{0,128},{4,132},{8,136},{12,140},{16,144},{20,148},{24,152},{28,15... | collective-permute-start | bytes 393224 | tf_op jit(solution)/shard_map/ppermute | solution.py:12
  362.2 6.2 %copy-start.35 = (s32[1024]{0:T(1024)S(1)}, s32[1024]{0:T(1024)}, u32[]{:S(2)}) copy-start(s32[1024]{0:T(1024)} %pad_clamp_fusion.3) | copy-start | bytes 12292
  370.0 9.1 %copy-start.37 = (s32[512]{0:T(512)S(1)}, s32[512]{0:T(512)}, u32[]{:S(2)}) copy-start(s32[512]{0:T(512)} %get-tuple-element.21) | copy-start | bytes 6148
  371.8 7.3 %copy-start.5 = (f32[1024,32]{1,0:T(8,128)S(1)}, f32[1024,32]{1,0:T(8,128)}, u32[]{:S(2)}) copy-start(f32[1024,32]{1,0:T(8,128)} %copy-done.4) | copy-start | bytes 393220
  375.0 8.4 %copy-start.12 = (f32[1024,32]{0,1:T(8,128)}, f32[1024,32]{0,1:T(8,128)S(1)}, u32[]{:S(2)}) copy-start(f32[1024,32]{0,1:T(8,128)S(1)} %fusion.7) | copy-start | bytes 393220
  375.0 8.4 %collective-permute-start.6 = (f32[1024,32]{0,1:T(8,128)S(1)}, f32[1024,32]{0,1:T(8,128)S(1)}, u32[]{:S(2)}, u32[]{:S(2)}) collective-permute-start(f32[1024,32]{0,1:T(8,128)S(1)} %fusion.7), channel_id=1, source_target_pairs={{0,256},{4,260},{8,264},{12,268},{16,272},{20,276},{24,280},{28,28... | collective-permute-start | bytes 393224 | tf_op jit(solution)/shard_map/ppermute | solution.py:12
  385.4 5.9 %copy-start.33 = (s32[1024]{0:T(1024)S(1)}, s32[1024]{0:T(1024)}, u32[]{:S(2)}) copy-start(s32[1024]{0:T(1024)} %pad_clamp_fusion.1) | copy-start | bytes 12292
  391.2 7.7 %copy-start.38 = (pred[1024]{0:T(1024)(128)(4,1)S(1)}, pred[1024]{0:T(1024)(128)(4,1)}, u32[]{:S(2)}) copy-start(pred[1024]{0:T(1024)(128)(4,1)} %compare_and_fusion) | copy-start | bytes 3076
  391.2 7.7 %copy-start.41 = (pred[512]{0:T(512)(128)(4,1)S(1)}, pred[512]{0:T(512)(128)(4,1)}, u32[]{:S(2)}) copy-start(pred[512]{0:T(512)(128)(4,1)} %get-tuple-element.18) | copy-start | bytes 1540
  392.9 6.1 %copy-start.44 = (pred[512]{0:T(512)(128)(4,1)S(1)}, pred[512]{0:T(512)(128)(4,1)}, u32[]{:S(2)}) copy-start(pred[512]{0:T(512)(128)(4,1)} %get-tuple-element.20) | copy-start | bytes 1540
  394.5 10.4 %all-to-all-start.2 = ((f32[4,256,32]{1,2,0:T(8,128)}), f32[4,256,32]{1,2,0:T(8,128)S(1)}, u32[]{:S(2)}, u32[]{:S(2)}) async-start(f32[4,256,32]{1,2,0:T(8,128)} %copy.240), calls=%async_computation.2 | async-start | bytes 262144 | tf_op jit(solution)/shard_map/all_to_all | solution.py:16
  404.9 9.3 %all-to-all-start.10 = ((f32[4,256,32]{1,2,0:T(8,128)}), f32[4,256,32]{1,2,0:T(8,128)S(1)}, u32[]{:S(2)}, u32[]{:S(2)}) async-start(f32[4,256,32]{1,2,0:T(8,128)} %bitcast.134), calls=%async_computation.10 | async-start | bytes 262144 | tf_op jit(solution)/shard_map/all_to_all | solution.py:16
  (18 other events, 48.5 us)
Sparse Core Ops, SparseCore 0:
  10.1 52.7 all-gather.4
